TPU v7x, 512 devices: a whole 4x4x16 slice. The times are simulated.
512 devices in a mesh: gx: 16 (over z), gy: 8 (over y, x_lo), gz: 4 (over x_hi, core).
Axes of the slice: x: 4 (x_hi: 2, x_lo: 2; x = x_hi * 2 + x_lo), y: 4, z: 16, core: 2. Of those that a mesh axis runs over, the one named last changes fastest.
Arguments:
- velocity: float32 [3, 128, 64, 512], P(None, 'gx', 'gy', 'gz'), may hold values from -4 to 4
- sketch_prev: float32 [3, 64, 4, 32, 32, 128], P(None, 'gy', 'gz', 'gx'), may hold values from -6 to 6
- seed_matrix: int32 [512, 128], replicated, may hold values from -4 to 4
- snap_steps: int32 [4], replicated, may hold values from 0 to 511
- rank_keep: int32 [1], replicated, may hold values from 32 to 128
Outputs:
- velocity_out: float32 [3, 128, 64, 512], P(None, 'gx', 'gy', 'gz')
- mode_rows: float32 [3, 64, 4, 32, 32, 128], P(None, 'gy', 'gz', 'gx')
- factor: float32 [128, 128], replicated
All inputs are finite; a program needn't handle non-finite values.
Results may differ from a plain program's by a relative error of at most 0.0003.
Values sent between devices are 32-bit elements; how exact they have to be, the bound alone decides.
No kernel may reach another device: no remote copies, remote signals or barrier semaphores. Data moves between devices by JAX's collectives and lax.ppermute only.
A program may use at most 64 MiB of HBM per device.

v0:
```python
import math
import jax
import jax.numpy as jnp
from jax import lax
from jax.sharding import PartitionSpec as P

SNAPS = 4
STEPS = 2
TIME_STEP = 0.1
VISCOSITY = 0.4
ONE_THIRD = 1.0 / 3.0
TWO_THIRDS = 2.0 / 3.0
HIGHEST = lax.Precision.HIGHEST


def extended(block, sides, width):
    for axis, dim in sides:
        count = lax.axis_size(axis)
        forward = [(i, i + 1) for i in range(count - 1)]
        forward.append((count - 1, 0))
        backward = [(target, source) for source, target in forward]
        low = lax.ppermute(
            lax.slice_in_dim(block, block.shape[dim] - width, None, axis=dim), axis, forward
        )
        high = lax.ppermute(lax.slice_in_dim(block, 0, width, axis=dim), axis, backward)
        block = jnp.concatenate([low, block, high], axis=dim)
    return block


def tendency(padded):
    center = padded[:, 1:-1, 1:-1, 1:-1]
    forward = (padded[:, 2:, 1:-1, 1:-1], padded[:, 1:-1, 2:, 1:-1], padded[:, 1:-1, 1:-1, 2:])
    backward = (padded[:, :-2, 1:-1, 1:-1], padded[:, 1:-1, :-2, 1:-1], padded[:, 1:-1, 1:-1, :-2])
    convect = (
        center[0:1] * (forward[0] - backward[0])
        + center[1:2] * (forward[1] - backward[1])
        + center[2:3] * (forward[2] - backward[2])
    )
    spread = (
        forward[0]
        + backward[0]
        + forward[1]
        + backward[1]
        + forward[2]
        + backward[2]
        - 6.0 * center
    )
    return -0.5 * convect + VISCOSITY * spread


def with_walls(padded, margin):
    cells_y = padded.shape[2] - 2 * margin
    wall_rows = (
        lax.axis_index("gy") * cells_y - margin + jnp.arange(cells_y + 2 * margin, dtype=jnp.int32)
    )
    inside = ((wall_rows >= 0) & (wall_rows < lax.axis_size("gy") * cells_y)).astype(jnp.float32)
    return padded * inside[None, None, :, None]


def faces_padded(current):
    return with_walls(extended(current, (("gx", 1), ("gy", 2), ("gz", 3)), 1), 1)


def step_by_section(current):
    first_section = current + TIME_STEP * tendency(faces_padded(current))
    second_section = 0.75 * current + 0.25 * (
        first_section + TIME_STEP * tendency(faces_padded(first_section))
    )
    return ONE_THIRD * current + TWO_THIRDS * (
        second_section + TIME_STEP * tendency(faces_padded(second_section))
    )


def coarse_local(current):
    cells_x = current.shape[1]
    cells_y = current.shape[2]
    cells_z = current.shape[3]
    blocks = current.reshape(3, cells_x // 4, 4, cells_y, cells_z // 4, 4)
    return jnp.transpose(jnp.mean(blocks, axis=(2, 5)), (0, 2, 3, 1))


def on_device(velocity, sketch_prev, seed_matrix, snap_steps, rank_keep):
    current = velocity
    collected = []
    for snap_index in range(SNAPS):
        for step_index in range(STEPS):
            current = step_by_section(current)
        local_snap = coarse_local(current)
        collected.append(lax.all_to_all(local_snap, "gx", split_axis=2, concat_axis=3, tiled=True))
    stacked = jnp.stack(collected)
    rank_total = sketch_prev.shape[-1]
    snap_rows = stacked.reshape(stacked.shape[0], -1)
    picker = (
        snap_steps[:, None] == jnp.arange(seed_matrix.shape[0], dtype=jnp.int32)[None, :]
    ).astype(jnp.float32)
    omega_rows = 0.5 * jnp.dot(picker, seed_matrix.astype(jnp.float32), precision=HIGHEST)
    sketch_rows = sketch_prev.reshape(-1, rank_total) + lax.dot_general(
        snap_rows, omega_rows, (((0,), (0,)), ((), ())), precision=HIGHEST
    )
    local_gram = lax.dot_general(
        sketch_rows, sketch_rows, (((0,), (0,)), ((), ())), precision=HIGHEST
    )
    gram_sum = lax.psum(local_gram, ("gx", "gy", "gz"))
    lower_factor = jnp.linalg.cholesky(gram_sum)
    identity = jnp.eye(rank_total, dtype=jnp.float32)
    inverse = lax.linalg.triangular_solve(lower_factor, identity, left_side=True, lower=True).T
    total_rows = (
        sketch_rows.shape[0] * lax.axis_size("gx") * lax.axis_size("gy") * lax.axis_size("gz")
    )
    norm_scale = math.sqrt(total_rows)
    inside = (jnp.arange(rank_total, dtype=jnp.int32) < rank_keep[0]).astype(jnp.float32)
    mode_rows = norm_scale * jnp.dot(sketch_rows, inverse, precision=HIGHEST) * inside[None, :]
    factor = lower_factor.T * (1.0 / norm_scale) * inside[:, None] * inside[None, :]
    return (current, mode_rows.reshape(sketch_prev.shape), factor)


def solution(mesh):
    placed = (P(None, "gx", "gy", "gz"), P(None, "gy", "gz", "gx", None, None), P(), P(), P())
    return jax.shard_map(
        on_device,
        mesh=mesh,
        in_specs=placed,
        out_specs=(P(None, "gx", "gy", "gz"), P(None, "gy", "gz", "gx", None, None), P()),
        check_vma=False,
    )
```

profile of v0, /device:TPU:1, one launch (start us, length us, event | category | flops | bytes accessed | tf_op | source)
XLA Modules:
  0.0 1293.1 jit_solution(17506120628596611169)
XLA Ops:
  12.3 9.5 collective-permute-start.1
  31.3 7.0 collective-permute-start.4
  41.4 5.9 collective-permute-done.5
  50.0 5.1 collective-permute-start.7
  71.5 5.9 collective-permute-done.11
  80.1 5.1 collective-permute-start.13
  88.3 5.2 collective-permute-start.15
  101.7 5.9 collective-permute-done.17
  110.4 5.0 collective-permute-start.19
  119.0 4.6 collective-permute-start.21
  131.8 5.9 collective-permute-done.23
  148.8 5.4 collective-permute-start.27
  162.7 5.9 collective-permute-done.29
  169.4 4.9 collective-permute-start.30
  181.3 5.1 collective-permute-start.33
  194.8 5.9 collective-permute-done.35
  211.8 5.5 collective-permute-start.39
  225.8 5.9 collective-permute-done.41
  242.5 5.5 collective-permute-start.45
  249.0 4.6 collective-permute-start.46
  256.7 5.9 collective-permute-done.47
  272.6 5.5 collective-permute-start.51
  279.1 4.6 collective-permute-start.52
  286.8 5.9 collective-permute-done.53
  303.0 5.5 collective-permute-start.57
  316.9 5.9 collective-permute-done.59
  333.2 5.4 collective-permute-start.63
  347.0 5.9 collective-permute-done.65
  363.3 5.5 collective-permute-start.69
  369.8 4.6 collective-permute-start.70
  377.5 5.9 collective-permute-done.71
  393.5 5.5 collective-permute-start.75
  400.0 4.6 collective-permute-start.76
  407.7 5.9 collective-permute-done.77
  423.9 5.5 collective-permute-start.81
  437.8 5.9 collective-permute-done.83
  454.1 5.4 collective-permute-start.87
  467.9 5.9 collective-permute-done.89
  484.1 5.5 collective-permute-start.93
  498.0 5.9 collective-permute-done.95
  514.2 5.5 collective-permute-start.99
  528.2 5.9 collective-permute-done.101
  544.4 5.5 collective-permute-start.105
  558.3 5.9 collective-permute-done.107
  574.5 5.5 collective-permute-start.111
  588.4 5.9 collective-permute-done.113
  604.9 5.7 collective-permute-start.117
  618.9 5.9 collective-permute-done.119
  635.8 5.5 collective-permute-start.123
  649.8 5.9 collective-permute-done.125
  666.8 5.5 collective-permute-start.129
  680.7 5.9 collective-permute-done.131
  697.7 5.5 collective-permute-start.135
  711.6 5.9 collective-permute-done.137
  725.5 6.0 all-to-all-start
  734.5 5.5 collective-permute-start.141
  748.1 5.9 collective-permute-done.143
  754.5 11.8 all-to-all-start.1
  767.5 11.1 all-to-all-done.1
  782.8 11.6 all-to-all-done.2
  801.6 8.7 all-to-all-done.3
  814.8 443.6 %all-reduce.2.cloned.1.call-done = f32[128,128]{0,1:T(8,128)} async-done(((f32[128,128]{0,1:T(8,128)}), f32[128,128]{0,1:T(8,128)}) %all-reduce.2.cloned.1.call-update) | async-done | bytes 65552 | tf_op jit(solution)/shard_map/psum | solution.py:103
  1260.2 11.7 cholesky.17
  1274.1 9.8 custom-call.6
  (461 shorter events, 445.5 us)
Async XLA Ops:
  8.0 13.9 %collective-permute-start = (f32[3,1,8,128]{3,2,1,0:T(8,128)S(1)}, f32[3,1,8,128]{3,2,1,0:T(8,128)S(1)}, u32[]{:S(2)}, u32[]{:S(2)}) collective-permute-start(f32[3,1,8,128]{3,2,1,0:T(8,128)S(1)} %get-tuple-element.230), channel_id=1, source_target_pairs={{0,32},{32,64},{64,96},{96,128},{128,160},{160,192},{192,224},{224... | collective-permute-start | bytes 36872 | tf_op jit(solution)/shard_map/ppermute | solution.py:22
  12.3 10.4 collective-permute-start.1
  22.8 7.5 collective-permute-start.2
  31.3 10.1 collective-permute-start.4
  38.3 9.0 collective-permute-start.5
  56.0 7.4 collective-permute-start.8
  68.4 9.0 collective-permute-start.11
  86.1 7.4 collective-permute-start.14
  98.5 9.0 collective-permute-start.17
  116.2 7.4 collective-permute-start.20
  128.7 9.0 collective-permute-start.23
  146.9 7.4 collective-permute-start.26
  155.3 7.4 collective-permute-start.28
  159.6 9.0 collective-permute-start.29
  187.4 7.4 collective-permute-start.34
  191.7 9.0 collective-permute-start.35
  218.3 7.4 collective-permute-start.40
  222.6 9.0 collective-permute-start.41
  249.0 7.7 collective-permute-start.46
  253.6 9.0 collective-permute-start.47
  270.7 7.4 collective-permute-start.50
  279.1 7.7 collective-permute-start.52
  283.7 9.0 collective-permute-start.53
  301.1 7.4 collective-permute-start.56
  309.5 7.4 collective-permute-start.58
  313.8 9.0 collective-permute-start.59
  331.2 7.4 collective-permute-start.62
  339.6 7.4 collective-permute-start.64
  343.9 9.0 collective-permute-start.65
  369.8 7.7 collective-permute-start.70
  374.4 9.0 collective-permute-start.71
  391.5 7.4 collective-permute-start.74
  400.0 7.7 collective-permute-start.76
  404.6 9.0 collective-permute-start.77
  430.4 7.4 collective-permute-start.82
  434.7 9.0 collective-permute-start.83
  460.5 7.4 collective-permute-start.88
  464.8 9.0 collective-permute-start.89
  490.6 7.4 collective-permute-start.94
  494.9 9.0 collective-permute-start.95
  520.7 7.4 collective-permute-start.100
  525.0 9.0 collective-permute-start.101
  550.9 7.4 collective-permute-start.106
  555.2 9.0 collective-permute-start.107
  581.0 7.4 collective-permute-start.112
  585.3 9.0 collective-permute-start.113
  603.0 7.6 collective-permute-start.116
  611.4 7.4 collective-permute-start.118
  615.8 9.0 collective-permute-start.119
  642.3 7.4 collective-permute-start.124
  646.7 9.0 collective-permute-start.125
  673.3 7.4 collective-permute-start.130
  677.6 9.0 collective-permute-start.131
  695.8 8.3 collective-permute-start.134
  708.5 9.0 collective-permute-start.137
  718.3 14.2 %collective-permute-start.138 = (f32[3,1,8,128]{3,2,1,0:T(8,128)S(1)}, f32[3,1,8,128]{3,2,1,0:T(8,128)S(1)}, u32[]{:S(2)}, u32[]{:S(2)}) collective-permute-start(f32[3,1,8,128]{3,2,1,0:T(8,128)S(1)} %get-tuple-element.183), channel_id=1, source_target_pairs={{0,32},{32,64},{64,96},{96,128},{128,160},{160,192},{192,224},{224... | collective-permute-start | bytes 36872 | tf_op jit(solution)/shard_map/ppermute | solution.py:22
  721.9 10.6 collective-permute-start.139
  725.5 29.0 %all-to-all-start = ((f32[3,8,32,2]{1,3,0,2:T(2,128)}), f32[3,8,32,2]{1,3,0,2:T(2,128)S(1)}, u32[]{:S(2)}, u32[]{:S(2)}) async-start(f32[3,8,32,2]{1,3,0,2:T(2,128)} %copy.41), calls=%async_computation | async-start | bytes 196608 | tf_op jit(solution)/shard_map/all_to_all | solution.py:89
  732.5 9.1 collective-permute-start.140
  745.0 9.0 collective-permute-start.143
  754.5 24.0 %all-to-all-start.1 = ((f32[3,8,32,2]{1,3,0,2:T(2,128)}), f32[3,8,32,2]{1,3,0,2:T(2,128)S(1)}, u32[]{:S(2)}, u32[]{:S(2)}) async-start(f32[3,8,32,2]{1,3,0,2:T(2,128)} %copy.45), calls=%async_computation.1 | async-start | bytes 196608 | tf_op jit(solution)/shard_map/all_to_all | solution.py:89
  778.6 15.8 %all-to-all-start.2 = ((f32[3,8,32,2]{1,3,0,2:T(2,128)}), f32[3,8,32,2]{1,3,0,2:T(2,128)S(1)}, u32[]{:S(2)}, u32[]{:S(2)}) async-start(f32[3,8,32,2]{1,3,0,2:T(2,128)} %copy.49), calls=%async_computation.2 | async-start | bytes 196608 | tf_op jit(solution)/shard_map/all_to_all | solution.py:89
  794.4 16.0 %all-to-all-start.3 = ((f32[3,8,32,2]{1,3,0,2:T(2,128)}), f32[3,8,32,2]{1,3,0,2:T(2,128)S(1)}, u32[]{:S(2)}, u32[]{:S(2)}) async-start(f32[3,8,32,2]{1,3,0,2:T(2,128)} %copy.53), calls=%async_computation.3 | async-start | bytes 196608 | tf_op jit(solution)/shard_map/all_to_all | solution.py:89
  798.5 459.9 %all-reduce.2.cloned.1.call-start = ((), (), s32[]{:S(2)}) async-start(), calls=%async_computation.4 | async-start | bytes 131072 | tf_op jit(solution)/shard_map/psum | solution.py:103
  (90 other events, 640.8 us)
Sparse Core Ops, SparseCore 0:
  814.9 443.4 all-reduce.1
where the time goes:
time: 1310 us; the launch traced here: 1290 us
  waiting for transfers between devices  687 us (52%)
  starting transfers between devices  523 us (40%)
  other arithmetic  42.5 us (3%)
  between operations  18.1 us (1%)
  local copies, waits for them, and re-layouts  17.1 us (1%)
    psum x1, waiting for transfers between devices, on_device(): gram_sum = lax.psum(local_gram, ('gx', 'gy', 'gz'))  444 us
    ppermute x72, starting transfers between devices, extended(): lax.ppermute(lax.slice_in_dim(block, 0, width, axis=dim), axis, backward)  267 us
    ppermute x72, starting transfers between devices, extended(): lax.ppermute(lax.slice_in_dim(block, block.shape[dim] - width, None, axis...  231 us
    ppermute x72, waiting for transfers between devices, extended(): lax.ppermute(lax.slice_in_dim(block, 0, width, axis=dim), axis, backward)  185 us
    all_to_all x4, waiting for transfers between devices, on_device(): lax.all_to_all(local_snap, 'gx', split_axis=2, concat_axis=3, tiled=True)  31.4 us
    ppermute x72, waiting for transfers between devices, extended(): lax.ppermute(lax.slice_in_dim(block, block.shape[dim] - width, None, axis...  26.8 us
  transfers between devices with their start and end apart: 149, of which 96 were waited for; matrix products, arithmetic and copies ran while one was open for 1% of the time, Pallas kernels for 0%

commit v1 on v0

--- a/solution.py
+++ b/solution.py
@@ -100,7 +100,8 @@
     local_gram = lax.dot_general(
         sketch_rows, sketch_rows, (((0,), (0,)), ((), ())), precision=HIGHEST
     )
-    gram_sum = lax.psum(local_gram, ("gx", "gy", "gz"))
+    parts = lax.all_gather(local_gram, ("gx", "gy", "gz"))
+    gram_sum = jnp.sum(parts, axis=0)
     lower_factor = jnp.linalg.cholesky(gram_sum)
     identity = jnp.eye(rank_total, dtype=jnp.float32)
     inverse = lax.linalg.triangular_solve(lower_factor, identity, left_side=True, lower=True).T

time: 1310 us -> 1720 us (1.31)
  waiting for transfers between devices: 687 us -> 1080 us
    all_gather x0 -> x1, waiting for transfers between devices: none -> 840 us  [on_device(): parts = lax.all_gather(local_gram, ('gx', 'gy', 'gz'))]
    psum x1 -> x0, waiting for transfers between devices: 444 us -> none  [on_device(): gram_sum = lax.psum(local_gram, ('gx', 'gy', 'gz'))]
  transfers between devices with their start and end apart: 149 -> 149, of which waited for: 96 -> 97; matrix products, arithmetic and copies ran while one was open for 1% -> 1% of each run, Pallas kernels for 0% -> 0%
where the time goes in v1:
time: 1720 us; the launch traced here: 1700 us
  waiting for transfers between devices  1080 us (63%)
  starting transfers between devices  523 us (30%)
  other arithmetic  54.9 us (3%)
  between operations  18.1 us (1%)
    all_gather x1, waiting for transfers between devices, on_device(): parts = lax.all_gather(local_gram, ('gx', 'gy', 'gz'))  840 us
    ppermute x72, starting transfers between devices, extended(): lax.ppermute(lax.slice_in_dim(block, 0, width, axis=dim), axis, backward)  267 us
    ppermute x72, starting transfers between devices, extended(): lax.ppermute(lax.slice_in_dim(block, block.shape[dim] - width, None, axis...  231 us
    ppermute x72, waiting for transfers between devices, extended(): lax.ppermute(lax.slice_in_dim(block, 0, width, axis=dim), axis, backward)  186 us
  transfers between devices with their start and end apart: 149, of which 97 were waited for; matrix products, arithmetic and copies ran while one was open for 1% of the time, Pallas kernels for 0%

profile of v1, /device:TPU:1, one launch (start us, length us, event | category | flops | bytes accessed | tf_op | source)
XLA Modules:
  0.0 1702.0 jit_solution(11728703029529781759)
XLA Ops:
  12.3 9.5 collective-permute-start.1
  31.3 7.0 collective-permute-start.4
  41.4 5.9 collective-permute-done.5
  50.0 5.1 collective-permute-start.7
  71.5 5.9 collective-permute-done.11
  80.1 5.1 collective-permute-start.13
  88.3 5.2 collective-permute-start.15
  101.7 5.9 collective-permute-done.17
  110.4 5.0 collective-permute-start.19
  119.0 4.6 collective-permute-start.21
  131.8 5.9 collective-permute-done.23
  148.8 5.4 collective-permute-start.27
  162.7 5.9 collective-permute-done.29
  169.4 4.9 collective-permute-start.30
  181.3 5.1 collective-permute-start.33
  194.8 5.9 collective-permute-done.35
  211.8 5.5 collective-permute-start.39
  225.8 5.9 collective-permute-done.41
  242.4 5.5 collective-permute-start.45
  248.9 4.6 collective-permute-start.46
  256.7 5.9 collective-permute-done.47
  272.6 5.5 collective-permute-start.51
  279.1 4.6 collective-permute-start.52
  286.8 5.9 collective-permute-done.53
  303.0 5.5 collective-permute-start.57
  316.9 5.9 collective-permute-done.59
  333.2 5.4 collective-permute-start.63
  347.0 5.9 collective-permute-done.65
  363.3 5.5 collective-permute-start.69
  369.8 4.6 collective-permute-start.70
  377.5 5.9 collective-permute-done.71
  393.4 5.5 collective-permute-start.75
  407.6 5.9 collective-permute-done.77
  423.8 5.5 collective-permute-start.81
  437.8 5.9 collective-permute-done.83
  454.0 5.4 collective-permute-start.87
  467.9 5.9 collective-permute-done.89
  484.1 5.5 collective-permute-start.93
  498.0 5.9 collective-permute-done.95
  514.2 5.5 collective-permute-start.99
  528.1 5.9 collective-permute-done.101
  544.3 5.5 collective-permute-start.105
  558.2 5.9 collective-permute-done.107
  574.4 5.5 collective-permute-start.111
  588.4 5.9 collective-permute-done.113
  604.9 5.7 collective-permute-start.117
  619.0 5.9 collective-permute-done.119
  636.0 5.5 collective-permute-start.123
  649.9 5.9 collective-permute-done.125
  666.9 5.5 collective-permute-start.129
  680.8 5.9 collective-permute-done.131
  697.8 5.5 collective-permute-start.135
  711.7 5.9 collective-permute-done.137
  725.6 6.0 all-to-all-start
  734.6 5.5 collective-permute-start.141
  748.2 5.9 collective-permute-done.143
  754.6 11.8 all-to-all-start.1
  767.6 11.0 all-to-all-done.1
  782.9 11.6 all-to-all-done.2
  801.9 8.5 all-to-all-done.3
  815.6 840.0 %all-gather.3.cloned.1.call-done = f32[65536,128]{1,0:T(8,128)} async-done(((f32[128,128]{1,0:T(8,128)}), f32[65536,128]{1,0:T(8,128)}) %all-gather.3.cloned.1.call-update) | async-done | bytes 33554448 | tf_op jit(solution)/shard_map/all_gather | solution.py:103
  1655.5 13.4 reduce_sum.49
  1669.0 11.7 cholesky.17
  1682.2 9.8 custom-call.6
  (460 shorter events, 449.4 us)
Async XLA Ops:
  8.0 13.9 collective-permute-start
  12.3 10.4 collective-permute-start.1
  22.8 7.5 collective-permute-start.2
  31.3 10.1 collective-permute-start.4
  38.3 9.0 collective-permute-start.5
  56.0 7.4 collective-permute-start.8
  68.4 9.0 collective-permute-start.11
  86.1 7.4 collective-permute-start.14
  98.5 9.0 collective-permute-start.17
  128.7 9.0 collective-permute-start.23
  155.3 7.4 collective-permute-start.28
  159.6 9.0 collective-permute-start.29
  179.0 7.4 collective-permute-start.32
  187.4 7.4 collective-permute-start.34
  191.7 9.0 collective-permute-start.35
  218.3 7.4 collective-permute-start.40
  222.6 9.0 collective-permute-start.41
  248.9 7.7 collective-permute-start.46
  253.5 9.0 collective-permute-start.47
  279.1 7.7 collective-permute-start.52
  283.7 9.0 collective-permute-start.53
  309.5 7.4 collective-permute-start.58
  313.8 9.0 collective-permute-start.59
  331.2 7.4 collective-permute-start.62
  339.6 7.4 collective-permute-start.64
  343.9 9.0 collective-permute-start.65
  369.8 7.7 collective-permute-start.70
  374.4 9.0 collective-permute-start.71
  399.9 7.7 collective-permute-start.76
  404.5 9.0 collective-permute-start.77
  430.3 7.4 collective-permute-start.82
  434.6 9.0 collective-permute-start.83
  452.0 7.4 collective-permute-start.86
  460.5 7.4 collective-permute-start.88
  464.8 9.0 collective-permute-start.89
  482.2 7.4 collective-permute-start.92
  490.6 7.4 collective-permute-start.94
  494.9 9.0 collective-permute-start.95
  520.7 7.4 collective-permute-start.100
  525.0 9.0 collective-permute-start.101
  550.8 7.4 collective-permute-start.106
  555.1 9.0 collective-permute-start.107
  580.9 7.4 collective-permute-start.112
  585.2 9.0 collective-permute-start.113
  603.0 7.6 collective-permute-start.116
  611.6 7.4 collective-permute-start.118
  615.9 9.0 collective-permute-start.119
  634.1 7.4 collective-permute-start.122
  642.5 7.4 collective-permute-start.124
  646.8 9.0 collective-permute-start.125
  665.0 7.4 collective-permute-start.128
  673.4 7.4 collective-permute-start.130
  677.7 9.0 collective-permute-start.131
  704.3 7.4 collective-permute-start.136
  708.6 9.0 collective-permute-start.137
  718.4 14.2 collective-permute-start.138
  722.0 10.6 collective-permute-start.139
  725.6 29.0 %all-to-all-start = ((f32[3,8,32,2]{1,3,0,2:T(2,128)}), f32[3,8,32,2]{1,3,0,2:T(2,128)S(1)}, u32[]{:S(2)}, u32[]{:S(2)}) async-start(f32[3,8,32,2]{1,3,0,2:T(2,128)} %copy.38), calls=%async_computation | async-start | bytes 196608 | tf_op jit(solution)/shard_map/all_to_all | solution.py:89
  732.6 9.1 collective-permute-start.140
  745.1 9.0 collective-permute-start.143
  754.6 24.0 %all-to-all-start.1 = ((f32[3,8,32,2]{1,3,0,2:T(2,128)}), f32[3,8,32,2]{1,3,0,2:T(2,128)S(1)}, u32[]{:S(2)}, u32[]{:S(2)}) async-start(f32[3,8,32,2]{1,3,0,2:T(2,128)} %copy.42), calls=%async_computation.1 | async-start | bytes 196608 | tf_op jit(solution)/shard_map/all_to_all | solution.py:89
  778.7 15.8 all-to-all-start.2
  794.5 16.0 all-to-all-start.3
  798.6 857.0 %all-gather.3.cloned.1.call-start = ((), (), s32[]{:S(2)}) async-start(), calls=%async_computation.4 | async-start | bytes 33619968 | tf_op jit(solution)/shard_map/all_gather | solution.py:103
  (90 other events, 644.2 us)
Sparse Core Ops, SparseCore 0:
  815.0 840.4 all-gather.2
